TPU v7x, 32 devices: a whole 2x2x4 slice. The times are simulated.
32 devices in a mesh: grp: 2 (over y), wide: 4 (over z), col: 2 (over x), inc: 2 (over core).
Axes of the slice: x: 2, y: 2, z: 4, core: 2. Of those that a mesh axis runs over, the one named last changes fastest.
Arguments:
- values_in: bfloat16 [32, 64, 256, 512], P(('grp', 'col'), 'inc', 'wide'), parts along dimension 0, may hold values from -6 to 6
- shock_load: float32 [32], P(('grp', 'col')), parts along dimension 0, may hold values from -4 to 4
- price_field: float32 [128, 256, 512], P(('grp', 'inc'), 'wide'), parts along dimension 0, may hold values from -6 to 6
- rate_liquid: float32 [128, 256, 512], P(('grp', 'inc'), 'wide'), parts along dimension 0, may hold values from 0.05 to 0.5
- rate_illiquid: float32 [128, 256, 512], P(('grp', 'inc'), 'wide'), parts along dimension 0, may hold values from 0.05 to 0.5
- mask_liquid: int32 [128, 256, 512], P(('grp', 'inc'), 'wide'), parts along dimension 0, may hold values 0 or 1
- mask_illiquid: int32 [128, 256, 512], P(('grp', 'inc'), 'wide'), parts along dimension 0, may hold values 0 or 1
- jump_inverse: float32 [128, 64], P('grp'), parts along dimension 0, may hold values from -0.07 to 0.87
- coef_liquid: int32 [4096], replicated, may hold values from 0 to 127, as said below
- coef_illiquid: int32 [4096], replicated, may hold values from 0 to 255
- coef_income: int32 [4096], replicated, may hold values from 0 to 63
- owner: int32 [4096], replicated, may hold values from 0 to 7, as said below
Outputs:
- reduced: float32 [32, 8192], P(('grp', 'col'), ('wide', 'inc')), parts along dimension 0
There are 2 independent parts, one for each index of `grp`. A program takes and returns all parts, laid end to end along the dimension named above; an argument that names none is the same for every part. Nothing has to cross between parts.
Inputs may be any that keep to these rules, and one draw needn't show every extreme that they name: `coef_liquid`: every retained coefficient has liquid frequency below 128. No owner has more than 1024 rows, and some owner has exactly 1024.
All inputs are finite; a program needn't handle non-finite values. No bound on the sum of `mask_liquid` or of `mask_illiquid` on one device may be relied on, other than what follows from the above.
Results may differ from a plain program's by a relative error of at most 0.0003.
Values may be sent and summed in bfloat16 or wider, within the bound.
No kernel may reach another device: no remote copies, remote signals or barrier semaphores. Data moves between devices by JAX's collectives and lax.ppermute only.
A program may use at most 256 MiB of HBM per device.

v0:
```python
import jax
import jax.numpy as jnp
from jax import lax
from jax.sharding import PartitionSpec as P

NB = 512
NA = 256
NZ = 64
KBLOW = 128


def padded_2(cells, sides, width):
    for axis, dim in sides:
        count = lax.axis_size(axis)
        ends = count - 1
        head = lax.slice_in_dim(cells, 0, width, axis=dim)
        tail = lax.slice_in_dim(cells, cells.shape[dim] - width, cells.shape[dim], axis=dim)
        cells = jnp.concatenate(
            [
                lax.ppermute(tail, axis, [(i, (i + 1) % count) for i in range(ends)]),
                cells,
                lax.ppermute(head, axis, [((i + 1) % count, i) for i in range(ends)]),
            ],
            axis=dim,
        )
    return cells


def cosine_table(count):
    freq = jnp.arange(count, dtype=jnp.int32)[:, None]
    cell = jnp.arange(count, dtype=jnp.int32)[None, :]
    phase = (2 * cell + 1) * freq % (4 * count)
    angle = jnp.pi * phase.astype(jnp.float32) / (2.0 * count)
    first = jnp.where(freq == 0, jnp.sqrt(jnp.float32(0.5)), jnp.float32(1.0))
    return jnp.cos(angle) * jnp.sqrt(jnp.float32(2.0 / count)) * first


def slot_targets(owner, owners, capacity):
    onehot = (owner[:, None] == jnp.arange(owners, dtype=jnp.int32)[None, :]).astype(jnp.int32)
    before = jnp.cumsum(onehot, axis=0) - onehot
    slot = jnp.sum(before * onehot, axis=1)
    return owner * capacity + slot


def body(
    values_in,
    shock_load,
    price_field,
    rate_liquid,
    rate_illiquid,
    mask_liquid,
    mask_illiquid,
    jump_inverse,
    coef_liquid,
    coef_illiquid,
    coef_income,
    owner,
):
    high = lax.Precision.HIGH
    columns, nz_loc, na_loc, _ = values_in.shape
    wide_pos = lax.axis_index("wide")
    inc_pos = lax.axis_index("inc")
    wide_count = lax.axis_size("wide")
    padded = padded_2(values_in, (("wide", 2),), 1).astype(jnp.float32)
    center = padded[:, :, 1:-1]
    lower = jnp.where(wide_pos == 0, center[:, :, 0:1], padded[:, :, 0:1])
    upper = jnp.where(wide_pos == wide_count - 1, center[:, :, -1:], padded[:, :, -1:])
    fwd_a = jnp.concatenate([center[:, :, 1:], upper], axis=2) - center
    bwd_a = center - jnp.concatenate([lower, center[:, :, :-1]], axis=2)
    step_b = center[:, :, :, 1:] - center[:, :, :, :-1]
    zero_b = jnp.zeros(center.shape[:3] + (1,), jnp.float32)
    fwd_b = jnp.concatenate([step_b, zero_b], axis=3)
    bwd_b = jnp.concatenate([zero_b, step_b], axis=3)
    mask_b = mask_liquid.astype(jnp.float32)
    mask_a = mask_illiquid.astype(jnp.float32)
    load = shock_load[:, None, None, None]
    explicit = (
        center
        + rate_liquid * (mask_b * fwd_b - (1.0 - mask_b) * bwd_b)
        + rate_illiquid * (mask_a * fwd_a - (1.0 - mask_a) * bwd_a)
        + load * price_field
    )
    table_b = cosine_table(NB)[:KBLOW]
    liquid_part = jnp.einsum("kb,czab->czak", table_b, explicit, precision=high)
    table_a = lax.dynamic_slice_in_dim(cosine_table(NA), wide_pos * na_loc, na_loc, axis=1)
    illiquid_part = jnp.einsum("ja,czak->jkcz", table_a, liquid_part, precision=high)
    rows = illiquid_part.reshape(NA * KBLOW, columns * nz_loc)
    picked = jnp.take(rows, coef_illiquid * KBLOW + coef_liquid, axis=0)
    folded = jnp.dot(cosine_table(NZ), jump_inverse, precision=lax.Precision.HIGHEST)
    folded = lax.dynamic_slice_in_dim(folded, inc_pos * nz_loc, nz_loc, axis=1)
    weight = jnp.take(folded, coef_income, axis=0)
    partial = jnp.sum(picked.reshape(-1, columns, nz_loc) * weight[:, None, :], axis=2)
    kept = lax.psum(partial, ("wide", "inc"))
    owners = lax.axis_size(("wide", "inc"))
    count = owner.shape[0]
    capacity = 2 * count // owners
    targets = slot_targets(owner, owners, capacity)
    source = (
        jnp.full((owners * capacity,), count, jnp.int32)
        .at[targets]
        .set(jnp.arange(count, dtype=jnp.int32))
    )
    mine = lax.dynamic_slice_in_dim(source, lax.axis_index(("wide", "inc")) * capacity, capacity)
    gathered = jnp.take(kept, jnp.minimum(mine, count - 1), axis=0)
    return jnp.where((mine < count)[None, :], gathered.T, jnp.float32(0.0))


def solution(mesh):
    placed = (
        P(("grp", "col"), "inc", "wide", None),
        P(("grp", "col")),
        P(("grp", "inc"), "wide", None),
        P(("grp", "inc"), "wide", None),
        P(("grp", "inc"), "wide", None),
        P(("grp", "inc"), "wide", None),
        P(("grp", "inc"), "wide", None),
        P("grp", None),
        P(),
        P(),
        P(),
        P(),
    )
    return jax.shard_map(
        body,
        mesh=mesh,
        in_specs=placed,
        out_specs=P(("grp", "col"), ("wide", "inc")),
        check_vma=False,
    )
```

profile of v0, /device:TPU:0, one launch (start us, length us, event | category | flops | bytes accessed | tf_op | source)
XLA Modules:
  0.0 500.5 jit_solution(14844286475312916411)
XLA Ops:
  6.6 3.3 fusion.94
  9.9 5.6 %collective-permute-start = (bf16[8,32,1,512]{3,1,2,0:T(8,128)(2,1)S(1)}, bf16[8,32,1,512]{3,1,2,0:T(8,128)(2,1)}, u32[]{:S(2)}, u32[]{:S(2)}) collective-permute-start(bf16[8,32,1,512]{3,1,2,0:T(8,128)(2,1)S(1)} %copy.34), channel_id=1, source_target_pairs={{0,4},{4,8},{8,12},{1,5},{5,9},{9,13},{2,6},{6,10},{10,14},{3,7},{... | collective-permute-start | bytes 786440 | tf_op jit(solution)/shard_map/ppermute | solution.py:20
  17.6 4.9 convert_element_type.28
  22.6 8.5 %broadcast_subtract_fusion = (f32[32,64,512]{2,1,0:T(8,128)}, f32[32,64,512]{2,1,0:T(8,128)}) fusion(s32[32,64,512]{2,1,0:T(8,128)} %param.18, s32[32,64,512]{2,1,0:T(8,128)} %param.17), kind=kLoop, calls=%fused_computation.39 | loop fusion | flops 4194304 | bytes 16777216 | tf_op jit(solution)/shard_map/sub | solution.py:80
  31.1 4.9 convert_element_type.29
  40.3 14.1 %gather_fusion.1 = f32[4096,32]{1,0:T(8,128)} fusion(f32[64,32]{1,0:T(8,128)S(1)} %copy.28, s32[4096]{0:T(1024)S(1)} %fusion.78), kind=kCustom, calls=%fused_computation.1 | custom fusion | bytes 1064960 | tf_op jit(solution)/shard_map/jit(_take)/gather | solution.py:91
  54.4 3.6 broadcast_select_fusion
  59.4 2.3 reduce-window.6
  62.5 15.5 %scatter_custom_fusion = s32[8192]{0:T(1024)S(1)} fusion(s32[4096]{0:T(1024)S(1)} %compare_select_fusion.2, s32[4096]{0:T(1024)S(1)} %iota.47, s32[]{:T(128)} %constant.66.clone.1), kind=kCustom, calls=%fused_computation.109 | custom fusion | bytes 32772 | tf_op jit(solution)/shard_map/scatter | solution.py:101
  82.0 20.9 %maximum_convert_fusion = f32[8,32,66,512]{3,2,1,0:T(8,128)} fusion(bf16[8,32,1,512]{3,2,1,0:T(2,128)(2,1)S(1)} %copy.24, bf16[8,32,64,512]{3,2,1,0:T(8,128)(2,1)} %param.12, bf16[8,32,1,512]{3,2,1,0:T(2,128)(2,1)S(1)} %copy.23), kind=kLoop, calls=%fused_computation.28 | loop fusion | flops 51904512 | bytes 51904512 | tf_op jit(solution)/shard_map/convert_element_type | solution.py:64
  102.9 47.7 %fusion.93 = (f32[8,32,63,512]{3,2,1,0:T(8,128)}, f32[8,32,63,512]{3,2,1,0:T(8,128)}) fusion(f32[8,32,66,512]{3,2,1,0:T(8,128)} %maximum_convert_fusion), kind=kLoop, calls=%fused_computation.140 | loop fusion | bytes 132120576 | tf_op jit(solution)/shard_map/slice | solution.py:69
  150.6 36.7 %slice_subtract_fusion = f32[8,32,64,511]{3,2,1,0:T(8,128)} fusion(f32[8,32,66,512]{3,2,1,0:T(8,128)} %maximum_convert_fusion), kind=kLoop, calls=%fused_computation.5 | loop fusion | flops 8372224 | bytes 100466688 | tf_op jit(solution)/shard_map/sub | solution.py:70
  187.3 4.8 broadcast_select_fusion.1
  192.2 73.0 %fusion.5 = f32[8,32,64,128]{3,2,1,0:T(8,128)} fusion(f32[8,32,1,512]{3,2,1,0:T(1,128)S(1)} %get-tuple-element.8, f32[8,32,63,512]{3,2,1,0:T(8,128)} %get-tuple-element.6, f32[8,32,63,512]{3,2,1,0:T(8,128)} %get-tuple-element.5, f32[8,32,1,512]{3,2,1,0:T(1,128)S(1)} %get-tuple-element.7, f32[8,32,66,512]{3,2,1,0:T(8,128)} %maximum_convert_fusion, ...), kind=kOutput, calls=%fused_computation.12 | convolution fusion | flops 6577061888 | bytes 173409280 | tf_op jit(solution)/shard_map/kb,czab->czak/dot_general | solution.py:84
  265.2 22.0 %convolution_bitcast_fusion = f32[256,128,8,32]{0,1,3,2:T(8,128)} fusion(f32[8,32,64,128]{3,2,1,0:T(8,128)} %fusion.5, s32[256,256]{0,1:T(8,128)} %negate_select_fusion.2, s32[]{:T(128)S(6)} %select_n.124, pred[256,256]{0,1:T(32,128)(4,1)} %get-tuple-element.16, pred[256,256]{0,1:T(32,128)(4,1)} %get-tuple-element.15, f32[256]{0:T(256)S(1)} %copy-done.14), kind=kOutput, calls=%fused_computation.37 | convolution fusion | flops 3221323776 | bytes 42042372 | tf_op jit(solution)/shard_map/ja,czak->jkcz/dot_general | solution.py:86
  287.3 31.1 %copy.25 = f32[256,128,8,32]{1,0,3,2:T(8,128)} copy(f32[256,128,8,32]{0,1,3,2:T(8,128)} %convolution_bitcast_fusion) | data formatting | bytes 67108864 | tf_op jit(solution)/shard_map/ja,czak->jkcz/transpose | solution.py:86
  318.4 31.8 %copy.40 = f32[32,8,256,128]{3,1,2,0:T(8,128)} copy(f32[32,8,256,128]{3,2,1,0:T(8,128)} %bitcast.48) | data formatting | bytes 67108864
  350.1 33.4 %copy.26 = f32[32768,256]{1,0:T(8,128)} copy(f32[32768,256]{0,1:T(8,128)} %bitcast.49) | data formatting | bytes 67108864 | tf_op jit(solution)/shard_map/reshape | solution.py:87
  383.6 26.7 %gather_fusion = f32[4096,256]{1,0:T(8,128)} fusion(f32[32768,256]{1,0:T(8,128)} %copy.26, s32[4096]{0:T(1024)S(1)} %copy-done.5), kind=kCustom, calls=%fused_computation | custom fusion | bytes 8404992 | tf_op jit(solution)/shard_map/jit(_take)/gather | solution.py:88
  410.3 5.6 %copy.27 = f32[4096,256]{0,1:T(8,128)} copy(f32[4096,256]{1,0:T(8,128)} %gather_fusion) | data formatting | bytes 8388608 | tf_op jit(solution)/shard_map/jit(_take)/gather | solution.py:88
  415.9 2.9 multiply_reduce_fusion
  418.8 1.9 copy.30
  421.5 66.6 %all-reduce.4.cloned.1.call-done = f32[4096,8]{1,0:T(8,128)} async-done(((f32[4096,8]{1,0:T(8,128)}), f32[4096,8]{1,0:T(8,128)}) %all-reduce.4.cloned.1.call-update) | async-done | bytes 131088 | tf_op jit(solution)/shard_map/psum | solution.py:93
  488.1 4.4 gather_fusion.2
  (70 shorter events, 14.3 us)
Async XLA Ops:
  6.5 33.3 %copy-start = (f32[64,64]{1,0:T(8,128)S(1)}, f32[64,64]{1,0:T(8,128)}, u32[]{:S(2)}) copy-start(f32[64,64]{1,0:T(8,128)} %param.19) | copy-start | bytes 49156
  6.5 31.8 %copy-start.8 = (s32[4096]{0:T(1024)S(1)}, s32[4096]{0:T(1024)}, u32[]{:S(2)}) copy-start(s32[4096]{0:T(1024)} %param.22) | copy-start | bytes 49156
  6.5 31.8 %copy-start.6 = (s32[4096]{0:T(1024)S(1)}, s32[4096]{0:T(1024)}, u32[]{:S(2)}) copy-start(s32[4096]{0:T(1024)} %param.20) | copy-start | bytes 49156
  6.5 31.8 %copy-start.7 = (s32[4096]{0:T(1024)S(1)}, s32[4096]{0:T(1024)}, u32[]{:S(2)}) copy-start(s32[4096]{0:T(1024)} %param.21) | copy-start | bytes 49156
  6.5 52.9 %copy-start.4 = (s32[4096]{0:T(1024)S(1)}, s32[4096]{0:T(1024)}, u32[]{:S(2)}) copy-start(s32[4096]{0:T(1024)} %param.23) | copy-start | bytes 49156
  6.5 481.5 %all-reduce.4.cloned.1.call-start = ((), (), s32[]{:S(2)}) async-start(), calls=%async_computation | async-start | bytes 4194304 | tf_op jit(solution)/shard_map/psum | solution.py:93
  9.9 69.3 %collective-permute-start = (bf16[8,32,1,512]{3,1,2,0:T(8,128)(2,1)S(1)}, bf16[8,32,1,512]{3,1,2,0:T(8,128)(2,1)}, u32[]{:S(2)}, u32[]{:S(2)}) collective-permute-start(bf16[8,32,1,512]{3,1,2,0:T(8,128)(2,1)S(1)} %copy.34), channel_id=1, source_target_pairs={{0,4},{4,8},{8,12},{1,5},{5,9},{9,13},{2,6},{6,10},{10,14},{3,7},{... | collective-permute-start | bytes 786440 | tf_op jit(solution)/shard_map/ppermute | solution.py:20
  16.3 64.3 %collective-permute-start.1 = (bf16[8,32,1,512]{3,1,2,0:T(8,128)(2,1)}, bf16[8,32,1,512]{3,1,2,0:T(8,128)(2,1)}, u32[]{:S(2)}, u32[]{:S(2)}) collective-permute-start(bf16[8,32,1,512]{3,1,2,0:T(8,128)(2,1)} %copy.35), channel_id=1, source_target_pairs={{4,0},{8,4},{12,8},{5,1},{9,5},{13,9},{6,2},{10,6},{14,10},{7,3},{... | collective-permute-start | bytes 786440 | tf_op jit(solution)/shard_map/ppermute | solution.py:22
  36.0 66.9 %copy-start.13 = (f32[512]{0:T(512)}, f32[512]{0:T(512)S(1)}, u32[]{:S(2)}) copy-start(f32[512]{0:T(512)S(1)} %select_multiply_fusion) | copy-start | bytes 6148
  78.0 72.6 %copy-start.9 = (s32[8192]{0:T(1024)}, s32[8192]{0:T(1024)S(1)}, u32[]{:S(2)}) copy-start(s32[8192]{0:T(1024)S(1)} %scatter_custom_fusion) | copy-start | bytes 98308
  150.6 41.6 %copy-start.10 = (f32[8]{0:T(128)S(1)}, f32[8]{0:T(128)}, u32[]{:S(2)}) copy-start(f32[8]{0:T(128)} %param.13) | copy-start | bytes 100
  150.6 41.6 %slice-start = ((f32[512]{0:T(512)}), f32[128]{0:T(128)S(1)}, s32[]{:S(2)}) async-start(f32[512]{0:T(512)} %copy-done.13), calls=%async_computation.1 | async-start | bytes 1024 | tf_op jit(solution)/shard_map/slice | solution.py:83
  187.3 4.9 copy-start.2
  192.2 73.0 %copy-start.14 = (f32[256]{0:T(256)S(1)}, f32[256]{0:T(256)}, u32[]{:S(2)}) copy-start(f32[256]{0:T(256)} %fusion.80) | copy-start | bytes 3076
  350.1 33.4 %copy-start.5 = (s32[4096]{0:T(1024)S(1)}, s32[4096]{0:T(1024)}, u32[]{:S(2)}) copy-start(s32[4096]{0:T(1024)} %broadcast_clamp_fusion) | copy-start | bytes 49156
  350.1 143.5 %copy-start.1 = (f32[64,64]{1,0:T(8,128)S(1)}, f32[64,64]{1,0:T(8,128)}, u32[]{:S(2)}) copy-start(f32[64,64]{1,0:T(8,128)} %param.19) | copy-start | bytes 49156
  383.6 32.3 %copy-start.3 = (f32[4096,32]{0,1:T(8,128)S(1)}, f32[4096,32]{0,1:T(8,128)}, u32[]{:S(2)}) copy-start(f32[4096,32]{0,1:T(8,128)} %copy.29) | copy-start | bytes 1572868
  383.6 32.3 %copy-start.11 = (pred[4096]{0:T(1024)(128)(4,1)S(1)}, pred[4096]{0:T(1024)(128)(4,1)}, u32[]{:S(2)}) copy-start(pred[4096]{0:T(1024)(128)(4,1)} %compare_and_fusion.1) | copy-start | bytes 12292
  383.6 104.5 %copy-start.12 = (s32[1024]{0:T(1024)S(1)}, s32[1024]{0:T(1024)}, u32[]{:S(2)}) copy-start(s32[1024]{0:T(1024)} %fusion.79) | copy-start | bytes 12292
Sparse Core Ops, SparseCore 0:
  420.9 67.1 all-reduce.3
where the time goes:
time: 502 us; the launch traced here: 500 us
  local copies, waits for them, and re-layouts  222 us (44%)
  other arithmetic  96.1 us (19%)
  matrix products  95.4 us (19%)
  waiting for transfers between devices  66.7 us (13%)
  between operations  13.7 us (3%)
  starting transfers between devices  6.96 us (1%)
    dot_general x1, matrix products, body(): liquid_part = jnp.einsum('kb,czab->czak', table_b, explicit, precision=high)  73 us
    psum x1, waiting for transfers between devices, body(): kept = lax.psum(partial, ('wide', 'inc'))  66.6 us
    slice x1, local copies, waits for them, and re-layouts, body(): bwd_a = center - jnp.concatenate([lower, center[:, :, :-1]], axis=2)  47.7 us
    sub x1, other arithmetic, body(): step_b = center[:, :, :, 1:] - center[:, :, :, :-1]  36.7 us
    reshape x1, local copies, waits for them, and re-layouts, body(): rows = illiquid_part.reshape(NA * KBLOW, columns * nz_loc)  33.4 us
    unnamed x33, local copies, waits for them, and re-layouts  32.6 us
    gather x2, local copies, waits for them, and re-layouts, body(): picked = jnp.take(rows, coef_illiquid * KBLOW + coef_liquid, axis=0)  32.3 us
    transpose x1, local copies, waits for them, and re-layouts, body(): jnp.einsum('ja,czak->jkcz', table_a, liquid_part, precision=high)  31.1 us
  transfers between devices with their start and end apart: 3, of which 1 were waited for; matrix products, arithmetic and copies ran while one was open for 13% of the time, Pallas kernels for 0%

commit v1 on v0

--- a/solution.py
+++ b/solution.py
@@ -7,6 +7,12 @@
 NA = 256
 NZ = 64
 KBLOW = 128
+
+
+def gather_and_add(x, axis):
+    shards = lax.all_gather(x, axis, axis=0, tiled=False)
+    total = shards.sum(axis=0)
+    return total
 
 
 def padded_2(cells, sides, width):
@@ -90,7 +96,7 @@
     folded = lax.dynamic_slice_in_dim(folded, inc_pos * nz_loc, nz_loc, axis=1)
     weight = jnp.take(folded, coef_income, axis=0)
     partial = jnp.sum(picked.reshape(-1, columns, nz_loc) * weight[:, None, :], axis=2)
-    kept = lax.psum(partial, ("wide", "inc"))
+    kept = gather_and_add(partial, ("wide", "inc"))
     owners = lax.axis_size(("wide", "inc"))
     count = owner.shape[0]
     capacity = 2 * count // owners

time: 502 us -> 439 us (0.87)
  waiting for transfers between devices: 66.7 us -> 5.96 us
    psum x1 -> x0, waiting for transfers between devices: 66.6 us -> none  [body(): kept = lax.psum(partial, ('wide', 'inc'))]
    all_gather x0 -> x1, waiting for transfers between devices: none -> 5.94 us  [gather_and_add(): shards = lax.all_gather(x, axis, axis=0, tiled=False)]
    unnamed x33 -> x29, local copies, waits for them, and re-layouts: 32.6 us -> 32.6 us
  transfers between devices with their start and end apart: 3 -> 3, of which waited for: 1 -> 1; matrix products, arithmetic and copies ran while one was open for 13% -> 14% of each run, Pallas kernels for 0% -> 0%
where the time goes in v1:
time: 439 us; the launch traced here: 437 us
  local copies, waits for them, and re-layouts  219 us (50%)
  other arithmetic  96.4 us (22%)
  matrix products  95.4 us (22%)
  between operations  13.7 us (3%)
  starting transfers between devices  6.95 us (2%)
  waiting for transfers between devices  5.96 us (1%)
    dot_general x1, matrix products, body(): liquid_part = jnp.einsum('kb,czab->czak', table_b, explicit, precision=high)  73.2 us
    slice x1, local copies, waits for them, and re-layouts, body(): bwd_a = center - jnp.concatenate([lower, center[:, :, :-1]], axis=2)  47.7 us
    sub x1, other arithmetic, body(): step_b = center[:, :, :, 1:] - center[:, :, :, :-1]  36.6 us
    reshape x1, local copies, waits for them, and re-layouts, body(): rows = illiquid_part.reshape(NA * KBLOW, columns * nz_loc)  33.5 us
    unnamed x29, local copies, waits for them, and re-layouts  32.6 us
    gather x2, local copies, waits for them, and re-layouts, body(): picked = jnp.take(rows, coef_illiquid * KBLOW + coef_liquid, axis=0)  32.3 us
    transpose x1, local copies, waits for them, and re-layouts, body(): jnp.einsum('ja,czak->jkcz', table_a, liquid_part, precision=high)  31.1 us
    dot_general x1, matrix products, body(): jnp.einsum('ja,czak->jkcz', table_a, liquid_part, precision=high)  21.8 us
  transfers between devices with their start and end apart: 3, of which 1 were waited for; matrix products, arithmetic and copies ran while one was open for 14% of the time, Pallas kernels for 0%

profile of v1, /device:TPU:0, one launch (start us, length us, event | category | flops | bytes accessed | tf_op | source)
XLA Modules:
  0.0 437.2 jit_solution(11128426106438819906)
XLA Ops:
  6.6 3.3 fusion.94
  9.9 5.6 %collective-permute-start = (bf16[8,32,1,512]{3,1,2,0:T(8,128)(2,1)S(1)}, bf16[8,32,1,512]{3,1,2,0:T(8,128)(2,1)}, u32[]{:S(2)}, u32[]{:S(2)}) collective-permute-start(bf16[8,32,1,512]{3,1,2,0:T(8,128)(2,1)S(1)} %copy.44), channel_id=1, source_target_pairs={{0,4},{4,8},{8,12},{1,5},{5,9},{9,13},{2,6},{6,10},{10,14},{3,7},{... | collective-permute-start | bytes 786440 | tf_op jit(solution)/shard_map/ppermute | solution.py:26
  17.6 4.9 %convert_element_type.28 = f32[32,64,512]{2,1,0:T(8,128)} convert(s32[32,64,512]{2,1,0:T(8,128)} %param.17) | non-fusion elementwise | flops 1048576 | bytes 8388608 | tf_op jit(solution)/shard_map/convert_element_type | solution.py:80
  22.5 8.5 %broadcast_subtract_fusion = (f32[32,64,512]{2,1,0:T(8,128)}, f32[32,64,512]{2,1,0:T(8,128)}) fusion(s32[32,64,512]{2,1,0:T(8,128)} %param.18, s32[32,64,512]{2,1,0:T(8,128)} %param.17), kind=kLoop, calls=%fused_computation.39 | loop fusion | flops 4194304 | bytes 16777216 | tf_op jit(solution)/shard_map/sub | solution.py:86
  31.1 4.9 %convert_element_type.29 = f32[32,64,512]{2,1,0:T(8,128)} convert(s32[32,64,512]{2,1,0:T(8,128)} %param.18) | non-fusion elementwise | flops 1048576 | bytes 8388608 | tf_op jit(solution)/shard_map/convert_element_type | solution.py:81
  40.3 14.1 %gather_fusion.1 = f32[4096,32]{1,0:T(8,128)} fusion(f32[64,32]{1,0:T(8,128)S(1)} %copy.38, s32[4096]{0:T(1024)S(1)} %fusion.78), kind=kCustom, calls=%fused_computation.1 | custom fusion | bytes 1064960 | tf_op jit(solution)/shard_map/jit(_take)/gather | solution.py:97
  54.3 3.6 broadcast_select_fusion
  57.9 1.4 copy.39
  62.7 20.7 %maximum_convert_fusion = f32[8,32,66,512]{3,2,1,0:T(8,128)} fusion(bf16[8,32,1,512]{3,2,1,0:T(2,128)(2,1)S(1)} %copy.34, bf16[8,32,64,512]{3,2,1,0:T(8,128)(2,1)} %param.12, bf16[8,32,1,512]{3,2,1,0:T(2,128)(2,1)S(1)} %copy.33), kind=kLoop, calls=%fused_computation.28 | loop fusion | flops 51904512 | bytes 51904512 | tf_op jit(solution)/shard_map/convert_element_type | solution.py:70
  83.5 47.7 %fusion.93 = (f32[8,32,63,512]{3,2,1,0:T(8,128)}, f32[8,32,63,512]{3,2,1,0:T(8,128)}) fusion(f32[8,32,66,512]{3,2,1,0:T(8,128)} %maximum_convert_fusion), kind=kLoop, calls=%fused_computation.140 | loop fusion | bytes 132120576 | tf_op jit(solution)/shard_map/slice | solution.py:75
  131.2 36.6 %slice_subtract_fusion = f32[8,32,64,511]{3,2,1,0:T(8,128)} fusion(f32[8,32,66,512]{3,2,1,0:T(8,128)} %maximum_convert_fusion), kind=kLoop, calls=%fused_computation.5 | loop fusion | flops 8372224 | bytes 100466688 | tf_op jit(solution)/shard_map/sub | solution.py:76
  167.8 4.8 %broadcast_select_fusion.1 = (f32[8,32,1,512]{3,2,1,0:T(1,128)S(1)}, f32[8,32,1,512]{3,2,1,0:T(1,128)S(1)}) fusion(pred[]{:T(512)S(6)} %eq.76, bf16[8,32,1,512]{3,2,1,0:T(2,128)(2,1)S(1)} %copy.34, bf16[8,32,64,512]{3,2,1,0:T(8,128)(2,1)} %param.12, bf16[8,32,1,512]{3,2,1,0:T(2,128)(2,1)S(1)} %copy.33, pred[]{:T(512)S(6)} %eq.75), kind=kLoop, calls=%fused_computation.45 | loop fusion | flops 3407872 | bytes 18350082 | tf_op jit(solution)/shard_map/jit(_where)/select_n | solution.py:72
  172.7 73.2 %fusion.5 = f32[8,32,64,128]{3,2,1,0:T(8,128)} fusion(f32[8,32,1,512]{3,2,1,0:T(1,128)S(1)} %get-tuple-element.8, f32[8,32,63,512]{3,2,1,0:T(8,128)} %get-tuple-element.6, f32[8,32,63,512]{3,2,1,0:T(8,128)} %get-tuple-element.5, f32[8,32,1,512]{3,2,1,0:T(1,128)S(1)} %get-tuple-element.7, f32[8,32,66,512]{3,2,1,0:T(8,128)} %maximum_convert_fusion, ...), kind=kOutput, calls=%fused_computation.12 | convolution fusion | flops 6577061888 | bytes 173409280 | tf_op jit(solution)/shard_map/kb,czab->czak/dot_general | solution.py:90
  245.9 21.8 %convolution_bitcast_fusion = f32[256,128,8,32]{0,1,3,2:T(8,128)} fusion(f32[8,32,64,128]{3,2,1,0:T(8,128)} %fusion.5, s32[256,256]{0,1:T(8,128)} %negate_select_fusion.2, s32[]{:T(128)S(6)} %select_n.124, pred[256,256]{0,1:T(32,128)(4,1)} %get-tuple-element.16, pred[256,256]{0,1:T(32,128)(4,1)} %get-tuple-element.15, f32[256]{0:T(256)S(1)} %copy-done.12), kind=kOutput, calls=%fused_computation.37 | convolution fusion | flops 3221323776 | bytes 42042372 | tf_op jit(solution)/shard_map/ja,czak->jkcz/dot_general | solution.py:92
  267.7 31.1 %copy.35 = f32[256,128,8,32]{1,0,3,2:T(8,128)} copy(f32[256,128,8,32]{0,1,3,2:T(8,128)} %convolution_bitcast_fusion) | data formatting | bytes 67108864 | tf_op jit(solution)/shard_map/ja,czak->jkcz/transpose | solution.py:92
  298.8 31.7 %copy.50 = f32[32,8,256,128]{3,1,2,0:T(8,128)} copy(f32[32,8,256,128]{3,2,1,0:T(8,128)} %bitcast.49) | data formatting | bytes 67108864
  330.5 33.5 %copy.36 = f32[32768,256]{1,0:T(8,128)} copy(f32[32768,256]{0,1:T(8,128)} %bitcast.50) | data formatting | bytes 67108864 | tf_op jit(solution)/shard_map/reshape | solution.py:93
  364.0 26.7 %gather_fusion = f32[4096,256]{1,0:T(8,128)} fusion(f32[32768,256]{1,0:T(8,128)} %copy.36, s32[4096]{0:T(1024)S(1)} %copy-done.5), kind=kCustom, calls=%fused_computation | custom fusion | bytes 8404992 | tf_op jit(solution)/shard_map/jit(_take)/gather | solution.py:94
  390.7 5.6 %copy.37 = f32[4096,256]{0,1:T(8,128)} copy(f32[4096,256]{1,0:T(8,128)} %gather_fusion) | data formatting | bytes 8388608 | tf_op jit(solution)/shard_map/jit(_take)/gather | solution.py:94
  396.3 3.5 multiply_reduce_fusion
  399.9 2.3 reduce-window.6
  403.0 15.5 %scatter_custom_fusion = s32[8192]{0:T(1024)S(1)} fusion(s32[4096]{0:T(1024)S(1)} %compare_select_fusion.2, s32[4096]{0:T(1024)S(1)} %iota.47, s32[]{:T(128)} %constant.66.clone.1), kind=kCustom, calls=%fused_computation.109 | custom fusion | bytes 32772 | tf_op jit(solution)/shard_map/scatter | solution.py:107
  418.6 5.9 %all-gather.3.cloned.1.call-done = f32[32768,8]{0,1:T(8,128)} async-done(((f32[4096,8]{0,1:T(8,128)}), f32[32768,8]{0,1:T(8,128)}) %all-gather.3.cloned.1.call-update) | async-done | bytes 1048592 | tf_op jit(solution)/shard_map/all_gather | solution.py:13
  426.4 2.8 gather_fusion.2
  (67 shorter events, 13.4 us)
Async XLA Ops:
  6.5 33.3 %copy-start = (f32[64,64]{1,0:T(8,128)S(1)}, f32[64,64]{1,0:T(8,128)}, u32[]{:S(2)}) copy-start(f32[64,64]{1,0:T(8,128)} %param.19) | copy-start | bytes 49156
  6.5 31.8 %copy-start.8 = (s32[4096]{0:T(1024)S(1)}, s32[4096]{0:T(1024)}, u32[]{:S(2)}) copy-start(s32[4096]{0:T(1024)} %param.22) | copy-start | bytes 49156
  6.5 31.8 %copy-start.6 = (s32[4096]{0:T(1024)S(1)}, s32[4096]{0:T(1024)}, u32[]{:S(2)}) copy-start(s32[4096]{0:T(1024)} %param.20) | copy-start | bytes 49156
  6.5 31.8 %copy-start.7 = (s32[4096]{0:T(1024)S(1)}, s32[4096]{0:T(1024)}, u32[]{:S(2)}) copy-start(s32[4096]{0:T(1024)} %param.21) | copy-start | bytes 49156
  6.5 418.0 %all-gather.3.cloned.1.call-start = ((), (), s32[]{:S(2)}) async-start(), calls=%async_computation | async-start | bytes 1179648 | tf_op jit(solution)/shard_map/all_gather | solution.py:13
  9.9 50.0 %collective-permute-start = (bf16[8,32,1,512]{3,1,2,0:T(8,128)(2,1)S(1)}, bf16[8,32,1,512]{3,1,2,0:T(8,128)(2,1)}, u32[]{:S(2)}, u32[]{:S(2)}) collective-permute-start(bf16[8,32,1,512]{3,1,2,0:T(8,128)(2,1)S(1)} %copy.44), channel_id=1, source_target_pairs={{0,4},{4,8},{8,12},{1,5},{5,9},{9,13},{2,6},{6,10},{10,14},{3,7},{... | collective-permute-start | bytes 786440 | tf_op jit(solution)/shard_map/ppermute | solution.py:26
  16.3 45.0 %collective-permute-start.1 = (bf16[8,32,1,512]{3,1,2,0:T(8,128)(2,1)}, bf16[8,32,1,512]{3,1,2,0:T(8,128)(2,1)}, u32[]{:S(2)}, u32[]{:S(2)}) collective-permute-start(bf16[8,32,1,512]{3,1,2,0:T(8,128)(2,1)} %copy.45), channel_id=1, source_target_pairs={{4,0},{8,4},{12,8},{5,1},{9,5},{13,9},{6,2},{10,6},{14,10},{7,3},{... | collective-permute-start | bytes 786440 | tf_op jit(solution)/shard_map/ppermute | solution.py:28
  36.0 47.4 %copy-start.11 = (f32[512]{0:T(512)}, f32[512]{0:T(512)S(1)}, u32[]{:S(2)}) copy-start(f32[512]{0:T(512)S(1)} %select_multiply_fusion) | copy-start | bytes 6148
  131.2 41.4 %copy-start.9 = (f32[8]{0:T(128)S(1)}, f32[8]{0:T(128)}, u32[]{:S(2)}) copy-start(f32[8]{0:T(128)} %param.13) | copy-start | bytes 100
  131.2 41.4 %slice-start = ((f32[512]{0:T(512)}), f32[128]{0:T(128)S(1)}, s32[]{:S(2)}) async-start(f32[512]{0:T(512)} %copy-done.11), calls=%async_computation.1 | async-start | bytes 1024 | tf_op jit(solution)/shard_map/slice | solution.py:89
  167.8 4.9 %copy-start.2 = (f32[32,64,512]{2,1,0:T(8,128)S(1)}, f32[32,64,512]{2,1,0:T(8,128)}, u32[]{:S(2)}) copy-start(f32[32,64,512]{2,1,0:T(8,128)} %convert_element_type.28) | copy-start | bytes 12582916
  172.7 73.2 %copy-start.12 = (f32[256]{0:T(256)S(1)}, f32[256]{0:T(256)}, u32[]{:S(2)}) copy-start(f32[256]{0:T(256)} %fusion.80) | copy-start | bytes 3076
  330.5 33.5 %copy-start.5 = (s32[4096]{0:T(1024)S(1)}, s32[4096]{0:T(1024)}, u32[]{:S(2)}) copy-start(s32[4096]{0:T(1024)} %broadcast_clamp_fusion) | copy-start | bytes 49156
  330.5 99.8 %copy-start.1 = (f32[64,64]{1,0:T(8,128)S(1)}, f32[64,64]{1,0:T(8,128)}, u32[]{:S(2)}) copy-start(f32[64,64]{1,0:T(8,128)} %param.19) | copy-start | bytes 49156
  364.0 32.3 %copy-start.3 = (f32[4096,32]{0,1:T(8,128)S(1)}, f32[4096,32]{0,1:T(8,128)}, u32[]{:S(2)}) copy-start(f32[4096,32]{0,1:T(8,128)} %copy.39) | copy-start | bytes 1572868
  364.0 32.3 %copy-start.10 = (pred[4096]{0:T(1024)(128)(4,1)S(1)}, pred[4096]{0:T(1024)(128)(4,1)}, u32[]{:S(2)}) copy-start(pred[4096]{0:T(1024)(128)(4,1)} %compare_and_fusion.1) | copy-start | bytes 12292
  364.0 35.9 %copy-start.4 = (s32[4096]{0:T(1024)S(1)}, s32[4096]{0:T(1024)}, u32[]{:S(2)}) copy-start(s32[4096]{0:T(1024)} %param.23) | copy-start | bytes 49156
Sparse Core Ops, SparseCore 0:
  400.0 24.4 all-gather.2
